TPU v7x, 512 devices: a whole 4x8x8 slice. The times are simulated.
512 devices in a mesh: seg: 16 (over z, x_lo), tok: 32 (over x_hi, y, core).
Axes of the slice: x: 4 (x_hi: 2, x_lo: 2; x = x_hi * 2 + x_lo), y: 8, z: 8, core: 2. Of those that a mesh axis runs over, the one named last changes fastest.
Arguments:
- seg_queries: bfloat16 [16, 4096, 2048], P('seg', 'tok'), may hold values from -8 to 8
- seg_keys: bfloat16 [16, 4096, 512], P('seg', 'tok'), may hold values from -8 to 8
- seg_values: bfloat16 [16, 4096, 512], P('seg', 'tok'), may hold values from -8 to 8
- grad_out: bfloat16 [16, 4096, 2048], P('seg', 'tok'), may hold values from -6 to 6
- mem_init: float32 [256, 1024], P('tok'), may hold values from -6 to 6
- mem_query: bfloat16 [256, 512], P('tok'), may hold values from -8 to 8
- retention: float32 [16, 1024], P('seg'), may hold values from 0 to 1
- seg_len: int32 [16], replicated, may hold values from 1024 to 4096, as said below
- doc_start: int32 [16], replicated, may hold values from 0 to 1, as said below
Outputs:
- attended: bfloat16 [16, 4096, 2048], P('seg', 'tok')
- memory_in: float32 [16, 256, 1024], P('seg', 'tok')
- memory_grad: float32 [16, 256, 1024], P('seg', 'tok')
Inputs may be any that keep to these rules, and one draw needn't show every extreme that they name: `seg_len`: A segment is full unless it is the last one of its document; segment 0 is always full and the last segment is the last one of its document. `doc_start`: segment 0 begins a document and segment 1 never does; any later segment may.
All inputs are finite; a program needn't handle non-finite values.
Results may differ from a plain program's by a relative error of at most 0.009.
Values may be sent and summed in bfloat16 or wider, within the bound.
No kernel may reach another device: no remote copies, remote signals or barrier semaphores. Data moves between devices by JAX's collectives and lax.ppermute only.
A program may use at most 64 MiB of HBM per device.

v0:
```python
import math

import jax
import jax.numpy as jnp
from jax import lax
from jax.sharding import PartitionSpec as P

HD = 128
QH = 16
KVH = 4


loss_scale = 16.0
neg_fill = -1e30
norm_eps = 1e-06


def shifted(block, axis, distance):
    devices = range(lax.axis_size(axis))
    route = [(i - distance, i) for i in devices if i - distance in devices]
    return lax.ppermute(block, axis, route)


def slot_norm(raw_rows):
    parts = raw_rows.reshape(raw_rows.shape[0], 2 * KVH, HD)
    multiplier = lax.rsqrt(jnp.mean(parts * parts, axis=-1, keepdims=True) + norm_eps)
    return (parts * multiplier).reshape(raw_rows.shape)


def softmax_step(row_top, row_total, scores, allowed):
    scores = jnp.where(allowed, scores, neg_fill)
    new_top = jnp.maximum(row_top, jnp.max(scores, axis=-1))
    weights = jnp.where(allowed, jnp.exp(scores - new_top[..., None]), 0.0)
    multiplier = jnp.exp(row_top - new_top)
    new_total = row_total * multiplier + jnp.sum(weights, axis=-1)
    return (new_top, new_total, weights.astype(jnp.bfloat16), multiplier)


def shards(
    seg_queries, seg_keys, seg_values, grad_out, mem_init, mem_query, retention, seg_len, doc_start
):
    tok_rows = seg_queries.shape[1]
    mem_rows = mem_query.shape[0]
    group_size = QH // KVH
    width_kv = KVH * HD
    seg_count = lax.axis_size("seg")
    seg_index = lax.axis_index("seg")
    tok_index = lax.axis_index("tok")
    length = seg_len[seg_index]
    score_scale = 1.0 / math.sqrt(HD)
    queries = seg_queries[0].reshape(tok_rows, KVH, group_size, HD)
    slot_queries = mem_query.reshape(mem_rows, KVH, HD)
    row_pos = tok_index * tok_rows + jnp.arange(tok_rows)
    starting = (
        jnp.full((KVH, group_size, tok_rows), neg_fill, jnp.float32),
        jnp.zeros((KVH, group_size, tok_rows), jnp.float32),
        jnp.zeros((tok_rows, KVH, group_size, HD), jnp.float32),
        jnp.full((KVH, mem_rows), neg_fill, jnp.float32),
        jnp.zeros((KVH, mem_rows), jnp.float32),
        jnp.zeros((mem_rows, KVH, HD), jnp.float32),
        jnp.zeros((mem_rows, KVH, HD), jnp.float32),
    )
    running = starting
    key_piece = lax.all_gather(seg_keys[0], "tok", axis=0, tiled=True)
    value_piece = lax.all_gather(seg_values[0], "tok", axis=0, tiled=True)
    piece_rows = key_piece.shape[0]
    block_rows = math.gcd(piece_rows, 512)
    blocks = piece_rows // block_rows
    key_blocks = key_piece.reshape(blocks, block_rows, KVH, HD)
    value_blocks = value_piece.reshape(blocks, block_rows, KVH, HD)
    block_first = block_rows * jnp.arange(blocks)

    def one_block(inner_state, inputs):
        key_block, value_block, block_start = inputs
        columns = block_start + jnp.arange(block_rows)
        live_keys = columns < length
        causal = (columns[None, :] <= row_pos[:, None]) & live_keys[None, :]
        seg_scores = (
            jnp.einsum("tgjd,ugd->gjtu", queries, key_block, preferred_element_type=jnp.float32)
            * score_scale
        )
        seg_top, seg_total, seg_weights, seg_factor = softmax_step(
            inner_state[0], inner_state[1], seg_scores, causal
        )
        seg_acc = inner_state[2] * jnp.transpose(seg_factor, (2, 0, 1))[..., None] + jnp.einsum(
            "gjtu,ugd->tgjd", seg_weights, value_block, preferred_element_type=jnp.float32
        )
        slot_scores = (
            jnp.einsum("rgd,ugd->gru", slot_queries, key_block, preferred_element_type=jnp.float32)
            * score_scale
        )
        slot_top, slot_total, slot_weights, slot_factor = softmax_step(
            inner_state[3], inner_state[4], slot_scores, live_keys
        )
        slot_scale = jnp.transpose(slot_factor)[..., None]
        slot_keys = inner_state[5] * slot_scale + jnp.einsum(
            "gru,ugd->rgd", slot_weights, key_block, preferred_element_type=jnp.float32
        )
        slot_values = inner_state[6] * slot_scale + jnp.einsum(
            "gru,ugd->rgd", slot_weights, value_block, preferred_element_type=jnp.float32
        )
        return ((seg_top, seg_total, seg_acc, slot_top, slot_total, slot_keys, slot_values), None)

    running, _ = lax.scan(one_block, running, (key_blocks, value_blocks, block_first))
    slot_denom = jnp.transpose(running[4])[..., None]
    raw_slots = jnp.concatenate(
        [
            (running[5] / slot_denom).reshape(mem_rows, width_kv),
            (running[6] / slot_denom).reshape(mem_rows, width_kv),
        ],
        axis=1,
    )
    written = slot_norm(raw_slots)
    ret_row = retention[0]
    following = doc_start[jnp.minimum(seg_index + 1, seg_count - 1)].astype(jnp.float32)
    keep_flag = jnp.where(seg_index == seg_count - 1, 1.0, 1.0 - following)
    decay_rate = keep_flag * ret_row
    carried = keep_flag * (1.0 - ret_row) * written + (1.0 - keep_flag) * mem_init

    def forward_turn(step_index, memory_now):
        moved = shifted(decay_rate * memory_now + carried, "seg", 1)
        return jnp.where(seg_index == 0, mem_init, moved)

    memory_in = lax.fori_loop(0, seg_count - 1, forward_turn, mem_init)
    memory_all = lax.all_gather(memory_in.astype(jnp.bfloat16), "tok", axis=0, tiled=True)
    mem_keys = memory_all[:, :width_kv].reshape(-1, KVH, HD)
    mem_vals = memory_all[:, width_kv:].reshape(-1, KVH, HD)
    mem_scores = (
        jnp.einsum("tgjd,mgd->gjtm", queries, mem_keys, preferred_element_type=jnp.float32)
        * score_scale
    )
    row_top = jnp.maximum(running[0], jnp.max(mem_scores, axis=-1))
    seg_factor = jnp.exp(running[0] - row_top)
    mem_weights = jnp.exp(mem_scores - row_top[..., None])
    row_total = running[1] * seg_factor + jnp.sum(mem_weights, axis=-1)
    weighted = running[2] * jnp.transpose(seg_factor, (2, 0, 1))[..., None] + jnp.einsum(
        "gjtm,mgd->tgjd",
        mem_weights.astype(jnp.bfloat16),
        mem_vals,
        preferred_element_type=jnp.float32,
    )
    att_rows = weighted / jnp.transpose(row_total, (2, 0, 1))[..., None]
    log_total = row_top + jnp.log(row_total)
    attended = att_rows.reshape(1, tok_rows, QH * HD).astype(jnp.bfloat16)
    valid_rows = (row_pos < length).astype(jnp.bfloat16)[:, None]
    cotangent = (grad_out[0] * valid_rows * loss_scale).reshape(tok_rows, KVH, group_size, HD)
    row_delta = jnp.einsum("tgjd,tgjd->gjt", cotangent.astype(jnp.float32), att_rows)
    mem_prob = jnp.exp(mem_scores - log_total[..., None])
    grad_prob = jnp.einsum(
        "tgjd,mgd->gjtm", cotangent, mem_vals, preferred_element_type=jnp.float32
    )
    grad_score = mem_prob * (grad_prob - row_delta[..., None])
    grad_vals = jnp.einsum(
        "gjtm,tgjd->mgd",
        mem_prob.astype(jnp.bfloat16),
        cotangent,
        preferred_element_type=jnp.float32,
    )
    grad_keys = (
        jnp.einsum(
            "gjtm,tgjd->mgd",
            grad_score.astype(jnp.bfloat16),
            queries,
            preferred_element_type=jnp.float32,
        )
        * score_scale
    )
    grad_slots = jnp.concatenate(
        [grad_keys.reshape(-1, width_kv), grad_vals.reshape(-1, width_kv)], axis=1
    )
    local_grad = lax.psum_scatter(grad_slots, "tok", scatter_dimension=0, tiled=True)

    def backward_turn(step_index, grad_now):
        moved = shifted(grad_now, "seg", -1)
        return local_grad + decay_rate * moved

    memory_grad = lax.fori_loop(0, seg_count - 1, backward_turn, local_grad)
    return (attended, memory_in[None], memory_grad[None])


def solution(mesh):
    placed = (
        P("seg", "tok", None),
        P("seg", "tok", None),
        P("seg", "tok", None),
        P("seg", "tok", None),
        P("tok", None),
        P("tok", None),
        P("seg", None),
        P(),
        P(),
    )
    return jax.shard_map(
        shards,
        mesh=mesh,
        in_specs=placed,
        out_specs=(P("seg", "tok", None), P("seg", "tok", None), P("seg", "tok", None)),
        check_vma=False,
    )
```

profile of v0, /device:TPU:218, one launch (start us, length us, event | category | flops | bytes accessed | tf_op | source)
XLA Modules:
  0.0 749.2 jit_solution(18313788783718589214)
XLA Ops:
  13.0 2.0 copy.90
  17.7 86.6 %all-gather.5.cloned.1.call-done = bf16[1,4096,512]{2,1,0:T(8,128)(2,1)} async-done(((bf16[1,128,512]{2,1,0:T(8,128)(2,1)}), bf16[1,4096,512]{2,1,0:T(8,128)(2,1)}) %all-gather.5.cloned.1.call-update) | async-done | bytes 4194320 | tf_op jit(solution)/shard_map/all_gather | solution.py:64
  104.2 6.9 reshape.119
  111.1 85.5 %all-gather.7.cloned.1.call-done = bf16[1,4096,512]{2,1,0:T(8,128)(2,1)} async-done(((bf16[1,128,512]{2,1,0:T(8,128)(2,1)}), bf16[1,4096,512]{2,1,0:T(8,128)(2,1)}) %all-gather.7.cloned.1.call-update) | async-done | bytes 4194320 | tf_op jit(solution)/shard_map/all_gather | solution.py:65
  196.6 6.9 reshape.120
  203.6 116.6 %while.47 = (s32[]{:T(128)}, f32[4,4,128]{2,1,0:T(4,128)S(1)}, f32[4,4,128]{2,1,0:T(4,128)S(1)}, f32[128,4,4,128]{0,3,2,1:T(8,128)}, f32[4,8]{1,0:T(4,128)S(1)},...) while((s32[]{:T(128)}, f32[4,4,128]{2,1,0:T(4,128)S(1)}, ...), condition=%wide.region_5.6_spmd.clone, body=%wide.region_0.5_spmd.clone.sunk | while | flops 564238208 | bytes 38488548 | solution.py:104
  208.0 2.8 fusion.109
  211.1 4.6 fusion.113
  222.3 2.8 fusion.109
  225.4 4.9 fusion.113
  236.9 2.8 fusion.109
  240.0 4.9 fusion.113
  251.5 2.8 fusion.109
  254.6 4.9 fusion.113
  266.2 2.8 fusion.109
  269.3 4.9 fusion.113
  280.8 2.8 fusion.109
  283.9 4.9 fusion.113
  295.4 2.8 fusion.109
  298.5 4.9 fusion.113
  310.0 2.8 fusion.109
  313.1 4.9 fusion.113
  320.4 118.5 %while.45 = (s32[]{:T(128)}, f32[8,1024]{1,0:T(8,128)S(1)}, pred[]{:T(512)}, f32[1024]{0:T(1024)S(1)}, f32[8,1024]{1,0:T(8,128)S(1)}, /*index=5*/f32[8,1024]{1,0:T(8,128)S(1)}, s32[]{:T(128)}) while((s32[]{:T(128)}, f32[8,1024]{1,0:T(8,128)S(1)}, pred[]{:T(512)}, f32[1024]{0:T(1024)S(1)}, f32[8,1024]{1,0:T(8,128)S(1)}, ...), condition=%wide.region_8.9_spmd, body=%wide.region_7.8_spmd.sunk | while | flops 24578 | bytes 331894 | solution.py:124
  320.4 5.7 collective-permute-start
  327.7 6.3 collective-permute-start
  335.6 6.3 collective-permute-start
  343.5 6.3 collective-permute-start
  351.5 6.3 collective-permute-start
  359.4 6.3 collective-permute-start
  367.4 6.4 collective-permute-start
  375.3 6.3 collective-permute-start
  383.3 6.3 collective-permute-start
  391.2 6.3 collective-permute-start
  399.1 6.3 collective-permute-start
  407.1 6.3 collective-permute-start
  415.0 6.5 collective-permute-start
  423.1 6.3 collective-permute-start
  431.0 6.3 collective-permute-start
  438.9 33.9 %all_gather.11 = bf16[256,1024]{1,0:T(8,128)(2,1)S(1)} all-gather(bf16[8,1024]{1,0:T(8,128)(2,1)S(1)} %convert_element_type.45), channel_id=1, replica_groups=mesh['seg'=16,'tok'=32] {'tok'}, dimensions={0}, use_global_device_ids=true | all-gather | bytes 540672 | tf_op jit(solution)/shard_map/all_gather | solution.py:125
  474.7 2.7 fusion.74
  485.2 125.7 %reduce-scatter.2.cloned.1.call-done = f32[8,1024]{1,0:T(8,128)} async-done(((f32[256,1024]{1,0:T(8,128)}), f32[8,1024]{1,0:T(8,128)}) %reduce-scatter.2.cloned.1.call-update) | async-done | bytes 32784 | tf_op jit(solution)/shard_map/reduce_scatter | solution.py:171
  611.6 130.4 %while.46 = (s32[]{:T(128)}, f32[8,1024]{1,0:T(8,128)S(1)}, f32[1024]{0:T(1024)S(1)}, f32[8,1024]{1,0:T(8,128)}, s32[]{:T(128)}) while((s32[]{:T(128)}, f32[8,1024]{1,0:T(8,128)S(1)}, f32[1024]{0:T(1024)S(1)}, f32[8,1024]{1,0:T(8,128)}, s32[]{:T(128)}) %tuple.103), condition=%wide.region_13.14_spmd, body=%wide.region_12.13_spmd.sunk | while | flops 16386 | bytes 233573 | solution.py:177
  611.6 2.8 collective-permute-start.1
  614.4 5.1 collective-permute-done.1
  620.3 1.9 collective-permute-start.1
  622.2 6.3 collective-permute-done.1
  629.3 1.9 collective-permute-start.1
  631.2 6.0 collective-permute-done.1
  637.9 1.9 collective-permute-start.1
  639.8 6.0 collective-permute-done.1
  646.6 1.9 collective-permute-start.1
  648.5 6.0 collective-permute-done.1
  655.3 1.9 collective-permute-start.1
  657.2 6.0 collective-permute-done.1
  664.0 1.9 collective-permute-start.1
  665.9 6.0 collective-permute-done.1
  674.5 6.0 collective-permute-done.1
  683.2 6.0 collective-permute-done.1
  691.9 6.0 collective-permute-done.1
  700.6 6.0 collective-permute-done.1
  709.3 6.0 collective-permute-done.1
  717.9 6.0 collective-permute-done.1
  726.6 6.0 collective-permute-done.1
  735.3 6.0 collective-permute-done.1
  (283 shorter events, 124.8 us)
Async XLA Ops:
  7.2 97.1 %all-gather.5.cloned.1.call-start = ((), (), s32[]{:S(2)}) async-start(), calls=%async_computation.2 | async-start | bytes 4325376 | tf_op jit(solution)/shard_map/all_gather | solution.py:64
  7.9 188.7 %all-gather.7.cloned.1.call-start = ((), (), s32[]{:S(2)}) async-start(), calls=%async_computation.3 | async-start | bytes 4325376 | tf_op jit(solution)/shard_map/all_gather | solution.py:65
  8.6 602.2 %reduce-scatter.2.cloned.1.call-start = ((), (), s32[]{:S(2)}) async-start(), calls=%async_computation.1 | async-start | bytes 1081344 | tf_op jit(solution)/shard_map/reduce_scatter | solution.py:171
  111.1 92.4 %copy-start.7 = (bf16[8,512]{1,0:T(8,128)(2,1)S(1)}, bf16[8,512]{1,0:T(8,128)(2,1)}, u32[]{:S(2)}) copy-start(bf16[8,512]{1,0:T(8,128)(2,1)} %param.20) | copy-start | bytes 24580
  203.6 116.8 %copy-start.3 = (f32[8,1024]{1,0:T(8,128)S(1)}, f32[8,1024]{1,0:T(8,128)}, u32[]{:S(2)}) copy-start(f32[8,1024]{1,0:T(8,128)} %param.19) | copy-start | bytes 98308
  211.1 4.6 copy-start
  225.4 4.9 copy-start
  240.0 4.9 copy-start
  254.6 4.9 copy-start
  269.2 4.9 copy-start
  283.9 4.9 copy-start
  298.5 4.9 copy-start
  313.1 4.9 copy-start
  320.4 7.2 collective-permute-start
  327.7 7.9 %collective-permute-start = (f32[8,1024]{1,0:T(8,128)S(1)}, f32[8,1024]{1,0:T(8,128)S(1)}, u32[]{:S(2)}, u32[]{:S(2)}) collective-permute-start(f32[8,1024]{1,0:T(8,128)S(1)} %multiply_add_fusion.5), channel_id=1, source_target_pairs={{0,32},{32,64},{64,96},{96,128},{128,160},{160,192},{192,224},{224... | collective-permute-start | bytes 98312 | tf_op jit(solution)/shard_map/while/body/eval_jaxpr/ppermute | solution.py:21
  335.6 7.9 %collective-permute-start = (f32[8,1024]{1,0:T(8,128)S(1)}, f32[8,1024]{1,0:T(8,128)S(1)}, u32[]{:S(2)}, u32[]{:S(2)}) collective-permute-start(f32[8,1024]{1,0:T(8,128)S(1)} %multiply_add_fusion.5), channel_id=1, source_target_pairs={{0,32},{32,64},{64,96},{96,128},{128,160},{160,192},{192,224},{224... | collective-permute-start | bytes 98312 | tf_op jit(solution)/shard_map/while/body/eval_jaxpr/ppermute | solution.py:21
  343.5 7.9 %collective-permute-start = (f32[8,1024]{1,0:T(8,128)S(1)}, f32[8,1024]{1,0:T(8,128)S(1)}, u32[]{:S(2)}, u32[]{:S(2)}) collective-permute-start(f32[8,1024]{1,0:T(8,128)S(1)} %multiply_add_fusion.5), channel_id=1, source_target_pairs={{0,32},{32,64},{64,96},{96,128},{128,160},{160,192},{192,224},{224... | collective-permute-start | bytes 98312 | tf_op jit(solution)/shard_map/while/body/eval_jaxpr/ppermute | solution.py:21
  351.5 7.9 %collective-permute-start = (f32[8,1024]{1,0:T(8,128)S(1)}, f32[8,1024]{1,0:T(8,128)S(1)}, u32[]{:S(2)}, u32[]{:S(2)}) collective-permute-start(f32[8,1024]{1,0:T(8,128)S(1)} %multiply_add_fusion.5), channel_id=1, source_target_pairs={{0,32},{32,64},{64,96},{96,128},{128,160},{160,192},{192,224},{224... | collective-permute-start | bytes 98312 | tf_op jit(solution)/shard_map/while/body/eval_jaxpr/ppermute | solution.py:21
  359.4 7.9 %collective-permute-start = (f32[8,1024]{1,0:T(8,128)S(1)}, f32[8,1024]{1,0:T(8,128)S(1)}, u32[]{:S(2)}, u32[]{:S(2)}) collective-permute-start(f32[8,1024]{1,0:T(8,128)S(1)} %multiply_add_fusion.5), channel_id=1, source_target_pairs={{0,32},{32,64},{64,96},{96,128},{128,160},{160,192},{192,224},{224... | collective-permute-start | bytes 98312 | tf_op jit(solution)/shard_map/while/body/eval_jaxpr/ppermute | solution.py:21
  367.4 8.0 %collective-permute-start = (f32[8,1024]{1,0:T(8,128)S(1)}, f32[8,1024]{1,0:T(8,128)S(1)}, u32[]{:S(2)}, u32[]{:S(2)}) collective-permute-start(f32[8,1024]{1,0:T(8,128)S(1)} %multiply_add_fusion.5), channel_id=1, source_target_pairs={{0,32},{32,64},{64,96},{96,128},{128,160},{160,192},{192,224},{224... | collective-permute-start | bytes 98312 | tf_op jit(solution)/shard_map/while/body/eval_jaxpr/ppermute | solution.py:21
  375.3 7.9 %collective-permute-start = (f32[8,1024]{1,0:T(8,128)S(1)}, f32[8,1024]{1,0:T(8,128)S(1)}, u32[]{:S(2)}, u32[]{:S(2)}) collective-permute-start(f32[8,1024]{1,0:T(8,128)S(1)} %multiply_add_fusion.5), channel_id=1, source_target_pairs={{0,32},{32,64},{64,96},{96,128},{128,160},{160,192},{192,224},{224... | collective-permute-start | bytes 98312 | tf_op jit(solution)/shard_map/while/body/eval_jaxpr/ppermute | solution.py:21
  383.3 7.9 %collective-permute-start = (f32[8,1024]{1,0:T(8,128)S(1)}, f32[8,1024]{1,0:T(8,128)S(1)}, u32[]{:S(2)}, u32[]{:S(2)}) collective-permute-start(f32[8,1024]{1,0:T(8,128)S(1)} %multiply_add_fusion.5), channel_id=1, source_target_pairs={{0,32},{32,64},{64,96},{96,128},{128,160},{160,192},{192,224},{224... | collective-permute-start | bytes 98312 | tf_op jit(solution)/shard_map/while/body/eval_jaxpr/ppermute | solution.py:21
  391.2 7.9 %collective-permute-start = (f32[8,1024]{1,0:T(8,128)S(1)}, f32[8,1024]{1,0:T(8,128)S(1)}, u32[]{:S(2)}, u32[]{:S(2)}) collective-permute-start(f32[8,1024]{1,0:T(8,128)S(1)} %multiply_add_fusion.5), channel_id=1, source_target_pairs={{0,32},{32,64},{64,96},{96,128},{128,160},{160,192},{192,224},{224... | collective-permute-start | bytes 98312 | tf_op jit(solution)/shard_map/while/body/eval_jaxpr/ppermute | solution.py:21
  399.1 7.9 %collective-permute-start = (f32[8,1024]{1,0:T(8,128)S(1)}, f32[8,1024]{1,0:T(8,128)S(1)}, u32[]{:S(2)}, u32[]{:S(2)}) collective-permute-start(f32[8,1024]{1,0:T(8,128)S(1)} %multiply_add_fusion.5), channel_id=1, source_target_pairs={{0,32},{32,64},{64,96},{96,128},{128,160},{160,192},{192,224},{224... | collective-permute-start | bytes 98312 | tf_op jit(solution)/shard_map/while/body/eval_jaxpr/ppermute | solution.py:21
  407.1 7.9 %collective-permute-start = (f32[8,1024]{1,0:T(8,128)S(1)}, f32[8,1024]{1,0:T(8,128)S(1)}, u32[]{:S(2)}, u32[]{:S(2)}) collective-permute-start(f32[8,1024]{1,0:T(8,128)S(1)} %multiply_add_fusion.5), channel_id=1, source_target_pairs={{0,32},{32,64},{64,96},{96,128},{128,160},{160,192},{192,224},{224... | collective-permute-start | bytes 98312 | tf_op jit(solution)/shard_map/while/body/eval_jaxpr/ppermute | solution.py:21
  415.0 8.1 %collective-permute-start = (f32[8,1024]{1,0:T(8,128)S(1)}, f32[8,1024]{1,0:T(8,128)S(1)}, u32[]{:S(2)}, u32[]{:S(2)}) collective-permute-start(f32[8,1024]{1,0:T(8,128)S(1)} %multiply_add_fusion.5), channel_id=1, source_target_pairs={{0,32},{32,64},{64,96},{96,128},{128,160},{160,192},{192,224},{224... | collective-permute-start | bytes 98312 | tf_op jit(solution)/shard_map/while/body/eval_jaxpr/ppermute | solution.py:21
  423.1 7.9 %collective-permute-start = (f32[8,1024]{1,0:T(8,128)S(1)}, f32[8,1024]{1,0:T(8,128)S(1)}, u32[]{:S(2)}, u32[]{:S(2)}) collective-permute-start(f32[8,1024]{1,0:T(8,128)S(1)} %multiply_add_fusion.5), channel_id=1, source_target_pairs={{0,32},{32,64},{64,96},{96,128},{128,160},{160,192},{192,224},{224... | collective-permute-start | bytes 98312 | tf_op jit(solution)/shard_map/while/body/eval_jaxpr/ppermute | solution.py:21
  431.0 7.9 %collective-permute-start = (f32[8,1024]{1,0:T(8,128)S(1)}, f32[8,1024]{1,0:T(8,128)S(1)}, u32[]{:S(2)}, u32[]{:S(2)}) collective-permute-start(f32[8,1024]{1,0:T(8,128)S(1)} %multiply_add_fusion.5), channel_id=1, source_target_pairs={{0,32},{32,64},{64,96},{96,128},{128,160},{160,192},{192,224},{224... | collective-permute-start | bytes 98312 | tf_op jit(solution)/shard_map/while/body/eval_jaxpr/ppermute | solution.py:21
  438.9 45.2 %copy-start.2 = (f32[8,1024]{1,0:T(8,128)}, f32[8,1024]{1,0:T(8,128)S(1)}, u32[]{:S(2)}) copy-start(f32[8,1024]{1,0:T(8,128)S(1)} %get-tuple-element.184) | copy-start | bytes 98308
  473.5 3.9 copy-start.1
  474.7 4.2 copy-start.5
  480.5 3.6 copy-start.4
  611.6 7.9 %collective-permute-start.1 = (f32[8,1024]{1,0:T(8,128)S(1)}, f32[8,1024]{1,0:T(8,128)S(1)}, u32[]{:S(2)}, u32[]{:S(2)}) collective-permute-start(f32[8,1024]{1,0:T(8,128)S(1)} %get-tuple-element.602), channel_id=1, source_target_pairs={{32,0},{64,32},{96,64},{128,96},{160,128},{192,160},{224,192},{256... | collective-permute-start | bytes 98312 | tf_op jit(solution)/shard_map/while/body/eval_jaxpr/ppermute | solution.py:21
  620.3 8.2 %collective-permute-start.1 = (f32[8,1024]{1,0:T(8,128)S(1)}, f32[8,1024]{1,0:T(8,128)S(1)}, u32[]{:S(2)}, u32[]{:S(2)}) collective-permute-start(f32[8,1024]{1,0:T(8,128)S(1)} %get-tuple-element.602), channel_id=1, source_target_pairs={{32,0},{64,32},{96,64},{128,96},{160,128},{192,160},{224,192},{256... | collective-permute-start | bytes 98312 | tf_op jit(solution)/shard_map/while/body/eval_jaxpr/ppermute | solution.py:21
  629.3 7.9 %collective-permute-start.1 = (f32[8,1024]{1,0:T(8,128)S(1)}, f32[8,1024]{1,0:T(8,128)S(1)}, u32[]{:S(2)}, u32[]{:S(2)}) collective-permute-start(f32[8,1024]{1,0:T(8,128)S(1)} %get-tuple-element.602), channel_id=1, source_target_pairs={{32,0},{64,32},{96,64},{128,96},{160,128},{192,160},{224,192},{256... | collective-permute-start | bytes 98312 | tf_op jit(solution)/shard_map/while/body/eval_jaxpr/ppermute | solution.py:21
  637.9 7.9 %collective-permute-start.1 = (f32[8,1024]{1,0:T(8,128)S(1)}, f32[8,1024]{1,0:T(8,128)S(1)}, u32[]{:S(2)}, u32[]{:S(2)}) collective-permute-start(f32[8,1024]{1,0:T(8,128)S(1)} %get-tuple-element.602), channel_id=1, source_target_pairs={{32,0},{64,32},{96,64},{128,96},{160,128},{192,160},{224,192},{256... | collective-permute-start | bytes 98312 | tf_op jit(solution)/shard_map/while/body/eval_jaxpr/ppermute | solution.py:21
  646.6 7.9 %collective-permute-start.1 = (f32[8,1024]{1,0:T(8,128)S(1)}, f32[8,1024]{1,0:T(8,128)S(1)}, u32[]{:S(2)}, u32[]{:S(2)}) collective-permute-start(f32[8,1024]{1,0:T(8,128)S(1)} %get-tuple-element.602), channel_id=1, source_target_pairs={{32,0},{64,32},{96,64},{128,96},{160,128},{192,160},{224,192},{256... | collective-permute-start | bytes 98312 | tf_op jit(solution)/shard_map/while/body/eval_jaxpr/ppermute | solution.py:21
  655.3 7.9 %collective-permute-start.1 = (f32[8,1024]{1,0:T(8,128)S(1)}, f32[8,1024]{1,0:T(8,128)S(1)}, u32[]{:S(2)}, u32[]{:S(2)}) collective-permute-start(f32[8,1024]{1,0:T(8,128)S(1)} %get-tuple-element.602), channel_id=1, source_target_pairs={{32,0},{64,32},{96,64},{128,96},{160,128},{192,160},{224,192},{256... | collective-permute-start | bytes 98312 | tf_op jit(solution)/shard_map/while/body/eval_jaxpr/ppermute | solution.py:21
  664.0 7.9 %collective-permute-start.1 = (f32[8,1024]{1,0:T(8,128)S(1)}, f32[8,1024]{1,0:T(8,128)S(1)}, u32[]{:S(2)}, u32[]{:S(2)}) collective-permute-start(f32[8,1024]{1,0:T(8,128)S(1)} %get-tuple-element.602), channel_id=1, source_target_pairs={{32,0},{64,32},{96,64},{128,96},{160,128},{192,160},{224,192},{256... | collective-permute-start | bytes 98312 | tf_op jit(solution)/shard_map/while/body/eval_jaxpr/ppermute | solution.py:21
  672.6 7.9 %collective-permute-start.1 = (f32[8,1024]{1,0:T(8,128)S(1)}, f32[8,1024]{1,0:T(8,128)S(1)}, u32[]{:S(2)}, u32[]{:S(2)}) collective-permute-start(f32[8,1024]{1,0:T(8,128)S(1)} %get-tuple-element.602), channel_id=1, source_target_pairs={{32,0},{64,32},{96,64},{128,96},{160,128},{192,160},{224,192},{256... | collective-permute-start | bytes 98312 | tf_op jit(solution)/shard_map/while/body/eval_jaxpr/ppermute | solution.py:21
  681.3 7.9 %collective-permute-start.1 = (f32[8,1024]{1,0:T(8,128)S(1)}, f32[8,1024]{1,0:T(8,128)S(1)}, u32[]{:S(2)}, u32[]{:S(2)}) collective-permute-start(f32[8,1024]{1,0:T(8,128)S(1)} %get-tuple-element.602), channel_id=1, source_target_pairs={{32,0},{64,32},{96,64},{128,96},{160,128},{192,160},{224,192},{256... | collective-permute-start | bytes 98312 | tf_op jit(solution)/shard_map/while/body/eval_jaxpr/ppermute | solution.py:21
  690.0 7.9 %collective-permute-start.1 = (f32[8,1024]{1,0:T(8,128)S(1)}, f32[8,1024]{1,0:T(8,128)S(1)}, u32[]{:S(2)}, u32[]{:S(2)}) collective-permute-start(f32[8,1024]{1,0:T(8,128)S(1)} %get-tuple-element.602), channel_id=1, source_target_pairs={{32,0},{64,32},{96,64},{128,96},{160,128},{192,160},{224,192},{256... | collective-permute-start | bytes 98312 | tf_op jit(solution)/shard_map/while/body/eval_jaxpr/ppermute | solution.py:21
  698.7 7.9 %collective-permute-start.1 = (f32[8,1024]{1,0:T(8,128)S(1)}, f32[8,1024]{1,0:T(8,128)S(1)}, u32[]{:S(2)}, u32[]{:S(2)}) collective-permute-start(f32[8,1024]{1,0:T(8,128)S(1)} %get-tuple-element.602), channel_id=1, source_target_pairs={{32,0},{64,32},{96,64},{128,96},{160,128},{192,160},{224,192},{256... | collective-permute-start | bytes 98312 | tf_op jit(solution)/shard_map/while/body/eval_jaxpr/ppermute | solution.py:21
  707.3 7.9 %collective-permute-start.1 = (f32[8,1024]{1,0:T(8,128)S(1)}, f32[8,1024]{1,0:T(8,128)S(1)}, u32[]{:S(2)}, u32[]{:S(2)}) collective-permute-start(f32[8,1024]{1,0:T(8,128)S(1)} %get-tuple-element.602), channel_id=1, source_target_pairs={{32,0},{64,32},{96,64},{128,96},{160,128},{192,160},{224,192},{256... | collective-permute-start | bytes 98312 | tf_op jit(solution)/shard_map/while/body/eval_jaxpr/ppermute | solution.py:21
  716.0 7.9 %collective-permute-start.1 = (f32[8,1024]{1,0:T(8,128)S(1)}, f32[8,1024]{1,0:T(8,128)S(1)}, u32[]{:S(2)}, u32[]{:S(2)}) collective-permute-start(f32[8,1024]{1,0:T(8,128)S(1)} %get-tuple-element.602), channel_id=1, source_target_pairs={{32,0},{64,32},{96,64},{128,96},{160,128},{192,160},{224,192},{256... | collective-permute-start | bytes 98312 | tf_op jit(solution)/shard_map/while/body/eval_jaxpr/ppermute | solution.py:21
  724.7 7.9 %collective-permute-start.1 = (f32[8,1024]{1,0:T(8,128)S(1)}, f32[8,1024]{1,0:T(8,128)S(1)}, u32[]{:S(2)}, u32[]{:S(2)}) collective-permute-start(f32[8,1024]{1,0:T(8,128)S(1)} %get-tuple-element.602), channel_id=1, source_target_pairs={{32,0},{64,32},{96,64},{128,96},{160,128},{192,160},{224,192},{256... | collective-permute-start | bytes 98312 | tf_op jit(solution)/shard_map/while/body/eval_jaxpr/ppermute | solution.py:21
  733.4 7.9 %collective-permute-start.1 = (f32[8,1024]{1,0:T(8,128)S(1)}, f32[8,1024]{1,0:T(8,128)S(1)}, u32[]{:S(2)}, u32[]{:S(2)}) collective-permute-start(f32[8,1024]{1,0:T(8,128)S(1)} %get-tuple-element.602), channel_id=1, source_target_pairs={{32,0},{64,32},{96,64},{128,96},{160,128},{192,160},{224,192},{256... | collective-permute-start | bytes 98312 | tf_op jit(solution)/shard_map/while/body/eval_jaxpr/ppermute | solution.py:21
  742.0 0.6 copy-start.6
Sparse Core Ops, SparseCore 0:
  11.3 92.8 all-gather.4
  107.6 88.9 all-gather.6
  484.3 126.5 reduce-scatter.1
where the time goes:
time: 753 us; the launch traced here: 749 us
  waiting for transfers between devices  412 us (55%)
  starting transfers between devices  124 us (16%)
  matrix products  73.9 us (10%)
  local copies, waits for them, and re-layouts  47 us (6%)
  other arithmetic  42.8 us (6%)
  blocking collectives  33.9 us (5%)
  between operations  14.6 us (2%)
    reduce_scatter x1, waiting for transfers between devices, shards(): lax.psum_scatter(grad_slots, 'tok', scatter_dimension=0, tiled=True)  126 us
    ppermute x30, starting transfers between devices, shifted(): return lax.ppermute(block, axis, route)  124 us
    ppermute x30, waiting for transfers between devices, shifted(): return lax.ppermute(block, axis, route)  113 us
    all_gather x1, waiting for transfers between devices, shards(): key_piece = lax.all_gather(seg_keys[0], 'tok', axis=0, tiled=True)  86.6 us
    all_gather x1, waiting for transfers between devices, shards(): value_piece = lax.all_gather(seg_values[0], 'tok', axis=0, tiled=True)  85.5 us
    dot_general x8, matrix products, one_block(): jnp.einsum('gjtu,ugd->tgjd', seg_weights, value_block, preferred_element_...  38.7 us
    all_gather x1, blocking collectives, shards(): lax.all_gather(memory_in.astype(jnp.bfloat16), 'tok', axis=0, tiled=True)  33.9 us
    dot_general x8, matrix products, one_block(): jnp.einsum('tgjd,ugd->gjtu', queries, key_block, preferred_element_type=j...  22.1 us
  transfers between devices with their start and end apart: 33, of which 33 were waited for; matrix products, arithmetic and copies ran while one was open for 2% of the time, Pallas kernels for 0%

commit v1 on v0

--- a/solution.py
+++ b/solution.py
@@ -13,12 +13,6 @@
 loss_scale = 16.0
 neg_fill = -1e30
 norm_eps = 1e-06
-
-
-def shifted(block, axis, distance):
-    devices = range(lax.axis_size(axis))
-    route = [(i - distance, i) for i in devices if i - distance in devices]
-    return lax.ppermute(block, axis, route)
 
 
 def slot_norm(raw_rows):
@@ -51,30 +45,69 @@
     queries = seg_queries[0].reshape(tok_rows, KVH, group_size, HD)
     slot_queries = mem_query.reshape(mem_rows, KVH, HD)
     row_pos = tok_index * tok_rows + jnp.arange(tok_rows)
-    starting = (
-        jnp.full((KVH, group_size, tok_rows), neg_fill, jnp.float32),
-        jnp.zeros((KVH, group_size, tok_rows), jnp.float32),
-        jnp.zeros((tok_rows, KVH, group_size, HD), jnp.float32),
-        jnp.full((KVH, mem_rows), neg_fill, jnp.float32),
-        jnp.zeros((KVH, mem_rows), jnp.float32),
-        jnp.zeros((mem_rows, KVH, HD), jnp.float32),
-        jnp.zeros((mem_rows, KVH, HD), jnp.float32),
+
+    kv_piece = lax.all_gather(
+        jnp.concatenate([seg_keys[0], seg_values[0]], axis=1), "tok", axis=0, tiled=True
     )
-    running = starting
-    key_piece = lax.all_gather(seg_keys[0], "tok", axis=0, tiled=True)
-    value_piece = lax.all_gather(seg_values[0], "tok", axis=0, tiled=True)
-    piece_rows = key_piece.shape[0]
+    piece_rows = kv_piece.shape[0]
+    key_piece = kv_piece[:, :width_kv].reshape(piece_rows, KVH, HD)
+    value_piece = kv_piece[:, width_kv:].reshape(piece_rows, KVH, HD)
+
+    live_keys = jnp.arange(piece_rows) < length
+    slot_scores = (
+        jnp.einsum("rgd,ugd->gru", slot_queries, key_piece, preferred_element_type=jnp.float32)
+        * score_scale
+    )
+    slot_scores = jnp.where(live_keys, slot_scores, neg_fill)
+    slot_top = jnp.max(slot_scores, axis=-1, keepdims=True)
+    slot_exp = jnp.where(live_keys, jnp.exp(slot_scores - slot_top), 0.0)
+    slot_denom = jnp.transpose(jnp.sum(slot_exp, axis=-1))[..., None]
+    slot_weights = slot_exp.astype(jnp.bfloat16)
+    slot_keys = jnp.einsum(
+        "gru,ugd->rgd", slot_weights, key_piece, preferred_element_type=jnp.float32
+    )
+    slot_values = jnp.einsum(
+        "gru,ugd->rgd", slot_weights, value_piece, preferred_element_type=jnp.float32
+    )
+    raw_slots = jnp.concatenate(
+        [
+            (slot_keys / slot_denom).reshape(mem_rows, width_kv),
+            (slot_values / slot_denom).reshape(mem_rows, width_kv),
+        ],
+        axis=1,
+    )
+    written = slot_norm(raw_slots)
+    ret_row = retention[0]
+    following = doc_start[jnp.minimum(seg_index + 1, seg_count - 1)].astype(jnp.float32)
+    keep_flag = jnp.where(seg_index == seg_count - 1, 1.0, 1.0 - following)
+    decay_rate = keep_flag * ret_row
+    carried = keep_flag * (1.0 - ret_row) * written + (1.0 - keep_flag) * mem_init
+
+    chain_terms = lax.all_gather(
+        jnp.concatenate([carried, decay_rate[None]], axis=0), "seg", axis=0, tiled=False
+    )
+    all_carried = chain_terms[:, :mem_rows]
+    all_decay = chain_terms[:, mem_rows]
+    memory_in = mem_init
+    for step in range(seg_count - 1):
+        following_memory = all_decay[step] * memory_in + all_carried[step]
+        memory_in = jnp.where(step < seg_index, following_memory, memory_in)
+
     block_rows = math.gcd(piece_rows, 512)
     blocks = piece_rows // block_rows
     key_blocks = key_piece.reshape(blocks, block_rows, KVH, HD)
     value_blocks = value_piece.reshape(blocks, block_rows, KVH, HD)
     block_first = block_rows * jnp.arange(blocks)
+    starting = (
+        jnp.full((KVH, group_size, tok_rows), neg_fill, jnp.float32),
+        jnp.zeros((KVH, group_size, tok_rows), jnp.float32),
+        jnp.zeros((tok_rows, KVH, group_size, HD), jnp.float32),
+    )
 
     def one_block(inner_state, inputs):
         key_block, value_block, block_start = inputs
         columns = block_start + jnp.arange(block_rows)
-        live_keys = columns < length
-        causal = (columns[None, :] <= row_pos[:, None]) & live_keys[None, :]
+        causal = (columns[None, :] <= row_pos[:, None]) & (columns < length)[None, :]
         seg_scores = (
             jnp.einsum("tgjd,ugd->gjtu", queries, key_block, preferred_element_type=jnp.float32)
             * score_scale
@@ -85,43 +118,10 @@
         seg_acc = inner_state[2] * jnp.transpose(seg_factor, (2, 0, 1))[..., None] + jnp.einsum(
             "gjtu,ugd->tgjd", seg_weights, value_block, preferred_element_type=jnp.float32
         )
-        slot_scores = (
-            jnp.einsum("rgd,ugd->gru", slot_queries, key_block, preferred_element_type=jnp.float32)
-            * score_scale
-        )
-        slot_top, slot_total, slot_weights, slot_factor = softmax_step(
-            inner_state[3], inner_state[4], slot_scores, live_keys
-        )
-        slot_scale = jnp.transpose(slot_factor)[..., None]
-        slot_keys = inner_state[5] * slot_scale + jnp.einsum(
-            "gru,ugd->rgd", slot_weights, key_block, preferred_element_type=jnp.float32
-        )
-        slot_values = inner_state[6] * slot_scale + jnp.einsum(
-            "gru,ugd->rgd", slot_weights, value_block, preferred_element_type=jnp.float32
-        )
-        return ((seg_top, seg_total, seg_acc, slot_top, slot_total, slot_keys, slot_values), None)
+        return ((seg_top, seg_total, seg_acc), None)
 
-    running, _ = lax.scan(one_block, running, (key_blocks, value_blocks, block_first))
-    slot_denom = jnp.transpose(running[4])[..., None]
-    raw_slots = jnp.concatenate(
-        [
-            (running[5] / slot_denom).reshape(mem_rows, width_kv),
-            (running[6] / slot_denom).reshape(mem_rows, width_kv),
-        ],
-        axis=1,
-    )
-    written = slot_norm(raw_slots)
-    ret_row = retention[0]
-    following = doc_start[jnp.minimum(seg_index + 1, seg_count - 1)].astype(jnp.float32)
-    keep_flag = jnp.where(seg_index == seg_count - 1, 1.0, 1.0 - following)
-    decay_rate = keep_flag * ret_row
-    carried = keep_flag * (1.0 - ret_row) * written + (1.0 - keep_flag) * mem_init
+    running, _ = lax.scan(one_block, starting, (key_blocks, value_blocks, block_first))
 
-    def forward_turn(step_index, memory_now):
-        moved = shifted(decay_rate * memory_now + carried, "seg", 1)
-        return jnp.where(seg_index == 0, mem_init, moved)
-
-    memory_in = lax.fori_loop(0, seg_count - 1, forward_turn, mem_init)
     memory_all = lax.all_gather(memory_in.astype(jnp.bfloat16), "tok", axis=0, tiled=True)
     mem_keys = memory_all[:, :width_kv].reshape(-1, KVH, HD)
     mem_vals = memory_all[:, width_kv:].reshape(-1, KVH, HD)
@@ -170,11 +170,11 @@
     )
     local_grad = lax.psum_scatter(grad_slots, "tok", scatter_dimension=0, tiled=True)
 
-    def backward_turn(step_index, grad_now):
-        moved = shifted(grad_now, "seg", -1)
-        return local_grad + decay_rate * moved
-
-    memory_grad = lax.fori_loop(0, seg_count - 1, backward_turn, local_grad)
+    all_local = lax.all_gather(local_grad, "seg", axis=0, tiled=False)
+    memory_grad = all_local[seg_count - 1]
+    for step in range(seg_count - 2, -1, -1):
+        earlier_grad = all_local[step] + all_decay[step] * memory_grad
+        memory_grad = jnp.where(step >= seg_index, earlier_grad, memory_grad)
     return (attended, memory_in[None], memory_grad[None])
 
 

time: 753 us -> 528 us (0.70)
  the two profiles are of different devices: /device:TPU:218 before, /device:TPU:16 now
where the time goes in v1:
time: 528 us; the launch traced here: 527 us
  waiting for transfers between devices  229 us (43%)
  blocking collectives  118 us (22%)
  matrix products  85 us (16%)
  local copies, waits for them, and re-layouts  45.9 us (9%)
  other arithmetic  32.6 us (6%)
  between operations  15 us (3%)
    reduce_scatter x1, waiting for transfers between devices, shards(): lax.psum_scatter(grad_slots, 'tok', scatter_dimension=0, tiled=True)  120 us
    all_gather x1, waiting for transfers between devices, shards(): lax.all_gather(jnp.concatenate([seg_keys[0], seg_values[0]], axis=1), 'to...  109 us
    all_gather x1, blocking collectives, shards(): lax.all_gather(jnp.concatenate([carried, decay_rate[None]], axis=0), 'seg...  41 us
    all_gather x1, blocking collectives, shards(): lax.all_gather(memory_in.astype(jnp.bfloat16), 'tok', axis=0, tiled=True)  40.3 us
    dot_general x8, matrix products, one_block(): jnp.einsum('gjtu,ugd->tgjd', seg_weights, value_block, preferred_element_...  39.5 us
    all_gather x1, blocking collectives, shards(): all_local = lax.all_gather(local_grad, 'seg', axis=0, tiled=False)  36.8 us
    dot_general x8, matrix products, one_block(): jnp.einsum('tgjd,ugd->gjtu', queries, key_block, preferred_element_type=j...  30 us
    unnamed x40, local copies, waits for them, and re-layouts  27.7 us
  transfers between devices with their start and end apart: 2, of which 2 were waited for; matrix products, arithmetic and copies ran while one was open for 2% of the time, Pallas kernels for 0%

profile of v1, /device:TPU:16, one launch (start us, length us, event | category | flops | bytes accessed | tf_op | source)
XLA Modules:
  0.0 526.6 jit_solution(17086343867945131486)
XLA Ops:
  7.2 1.0 copy.115
  8.3 1.0 copy.116
  10.1 1.2 dynamic_slice.18
  12.1 1.3 copy.117
  13.7 2.1 copy.163
  16.5 1.2 compare_convert_fusion
  18.4 108.9 %all-gather.5.cloned.1.call-done = bf16[4096,1024]{0,1:T(8,128)(2,1)} async-done(((bf16[128,1024]{0,1:T(8,128)(2,1)}), bf16[4096,1024]{0,1:T(8,128)(2,1)}) %all-gather.5.cloned.1.call-update) | async-done | bytes 8388624 | tf_op jit(solution)/shard_map/all_gather | solution.py:49
  127.3 5.9 %fusion.131 = (bf16[4096,512]{0,1:T(8,128)(2,1)}, bf16[4096,512]{0,1:T(8,128)(2,1)}) fusion(bf16[4096,1024]{0,1:T(8,128)(2,1)} %all-gather.5.cloned.1.call-done), kind=kLoop, calls=%fused_computation.186 | loop fusion | bytes 16777216 | tf_op jit(solution)/shard_map/slice | solution.py:53
  133.2 3.1 fusion.134
  136.3 3.5 fusion.45
  139.9 1.2 fusion.44
  141.3 41.0 %all-gather.2 = f32[16,9,1024]{2,1,0:T(8,128)S(1)} all-gather(f32[1,9,1024]{2,1,0:T(8,128)S(1)} %maximum_bitcast_fusion), channel_id=2, replica_groups=mesh['seg'=16,'tok'=32] {'seg'}, dimensions={0}, use_global_device_ids=true | all-gather | bytes 626688 | tf_op jit(solution)/shard_map/all_gather | solution.py:86
  182.3 0.7 fusion.129
  183.1 40.3 %all_gather.21 = bf16[256,1024]{1,0:T(8,128)(2,1)S(1)} all-gather(bf16[8,1024]{1,0:T(8,128)(2,1)S(1)} %get-tuple-element.175), channel_id=1, replica_groups=mesh['seg'=16,'tok'=32] {'tok'}, dimensions={0}, use_global_device_ids=true | all-gather | bytes 540672 | tf_op jit(solution)/shard_map/all_gather | solution.py:125
  223.5 0.8 copy.165
  224.3 2.0 bitcast_reduce_fusion
  226.3 6.4 %copy.166 = bf16[64,8,8,512]{3,2,1,0:T(8,128)(2,1)} copy(bf16[64,8,8,512]{3,1,2,0:T(8,128)(2,1)} %bitcast.463) | data formatting | bytes 8388608
  232.7 7.9 %copy.118 = bf16[8,512,4,128]{3,1,2,0:T(8,128)(2,1)} copy(bf16[8,512,4,128]{1,0,3,2:T(8,128)(2,1)} %bitcast.464) | data formatting | bytes 8388608
  240.6 4.4 copy.167
  245.1 3.4 copy.120
  248.5 100.9 %while.15 = (s32[]{:T(128)}, f32[4,4,128]{2,1,0:T(4,128)S(1)}, f32[4,4,128]{2,1,0:T(4,128)S(1)}, f32[128,4,4,128]{0,3,2,1:T(8,128)}, s32[8]{0:T(128)S(1)}, /*ind...) while((s32[]{:T(128)}, f32[4,4,128]{2,1,0:T(4,128)S(1)}, ...), condition=%wide.region_3.4_spmd.clone, body=%wide.region_0.3_spmd.clone.sunk | while | flops 551433856 | bytes 33431024 | solution.py:123
  249.1 1.3 broadcast_compare_fusion.2
  251.3 3.8 fusion.160
  255.1 4.7 fusion.164
  259.8 1.0 fusion.162
  261.4 1.3 broadcast_compare_fusion.2
  263.6 3.8 fusion.160
  267.4 5.0 fusion.164
  272.4 1.0 fusion.162
  274.1 1.3 broadcast_compare_fusion.2
  276.3 3.8 fusion.160
  280.1 5.0 fusion.164
  285.1 1.0 fusion.162
  286.7 1.3 broadcast_compare_fusion.2
  288.9 3.8 fusion.160
  292.7 5.0 fusion.164
  297.7 1.0 fusion.162
  299.4 1.3 broadcast_compare_fusion.2
  301.6 3.8 fusion.160
  305.4 5.0 fusion.164
  310.3 1.0 fusion.162
  312.0 1.3 broadcast_compare_fusion.2
  314.2 3.8 fusion.160
  318.0 5.0 fusion.164
  323.0 1.0 fusion.162
  324.7 1.3 broadcast_compare_fusion.2
  326.9 3.8 fusion.160
  330.7 5.0 fusion.164
  335.6 1.0 fusion.162
  337.3 1.3 broadcast_compare_fusion.2
  339.5 3.8 fusion.160
  343.3 5.0 fusion.164
  348.3 1.0 fusion.162
  349.4 0.8 copy.127
  351.3 2.7 fusion.135
  354.2 1.3 fusion.47
  355.4 1.7 fusion.43
  357.2 1.3 copy.134
  358.5 1.2 copy.135
  359.7 1.1 pad_maximum_fusion
  360.8 1.0 copy.136
  361.9 120.3 %reduce-scatter.2.cloned.1.call-done = f32[8,1024]{1,0:T(8,128)} async-done(((f32[256,1024]{1,0:T(8,128)}), f32[8,1024]{1,0:T(8,128)}) %reduce-scatter.2.cloned.1.call-update) | async-done | bytes 32784 | tf_op jit(solution)/shard_map/reduce_scatter | solution.py:171
  482.2 36.8 %all-gather.1 = f32[128,1024]{1,0:T(8,128)S(1)} all-gather(f32[8,1024]{1,0:T(8,128)} %reduce-scatter.2.cloned.1.call-done), channel_id=3, replica_groups=mesh['seg'=16,'tok'=32] {'seg'}, dimensions={0}, use_global_device_ids=true | all-gather | bytes 557056 | tf_op jit(solution)/shard_map/all_gather | solution.py:173
  519.1 0.7 fusion.91
  (157 shorter events, 16.0 us)
Async XLA Ops:
  7.2 126.1 %copy-start = (bf16[8,512]{1,0:T(8,128)(2,1)S(1)}, bf16[8,512]{1,0:T(8,128)(2,1)}, u32[]{:S(2)}) copy-start(bf16[8,512]{1,0:T(8,128)(2,1)} %param.16) | copy-start | bytes 24580
  7.2 8.6 %copy-start.15 = (s32[16]{0:T(128)S(1)}, s32[16]{0:T(128)}, u32[]{:S(2)}) copy-start(s32[16]{0:T(128)} %param.18) | copy-start | bytes 196
  7.2 11.2 %copy-start.13 = (f32[1,1024]{1,0:T(1,128)S(1)}, f32[1,1024]{1,0:T(1,128)}, u32[]{:S(2)}) copy-start(f32[1,1024]{1,0:T(1,128)} %param.17) | copy-start | bytes 12292
  7.2 120.1 %all-gather.5.cloned.1.call-start = ((), (), s32[]{:S(2)}) async-start(), calls=%async_computation.1 | async-start | bytes 8650752 | tf_op jit(solution)/shard_map/all_gather | solution.py:49
  10.1 472.2 %reduce-scatter.2.cloned.1.call-start = ((), (), s32[]{:S(2)}) async-start(), calls=%async_computation.2 | async-start | bytes 1081344 | tf_op jit(solution)/shard_map/reduce_scatter | solution.py:171
  136.3 3.5 copy-start.2
  136.3 4.8 copy-start.6
  182.3 0.8 copy-start.7
  182.3 0.8 copy-start.9
  182.3 0.8 copy-start.11
  248.5 0.6 copy-start.16
  255.1 4.7 copy-start.1
  259.8 1.1 copy-start.17
  260.8 0.6 copy-start.16
  267.4 5.0 copy-start.1
  272.4 1.1 copy-start.17
  273.5 0.6 copy-start.16
  280.1 5.0 copy-start.1
  285.0 1.1 copy-start.17
  286.1 0.6 copy-start.16
  292.7 5.0 copy-start.1
  297.7 1.1 copy-start.17
  298.8 0.6 copy-start.16
  305.4 5.0 copy-start.1
  310.3 1.1 copy-start.17
  311.4 0.6 copy-start.16
  318.0 5.0 copy-start.1
  323.0 1.1 copy-start.17
  324.1 0.6 copy-start.16
  330.7 5.0 copy-start.1
  335.6 1.1 copy-start.17
  336.7 0.6 copy-start.16
  343.3 5.0 copy-start.1
  348.3 1.1 copy-start.17
  349.4 4.6 copy-start.3
  349.4 4.6 copy-start.14
  351.2 4.2 copy-start.5
  357.2 3.7 copy-start.4
  357.2 161.9 %copy-start.8 = (f32[1,1,1024]{2,1,0:T(1,128)S(1)}, f32[1,1,1024]{2,1,0:T(1,128)}, u32[]{:S(2)}) copy-start(f32[1,1,1024]{2,1,0:T(1,128)} %copy-done.7) | copy-start | bytes 12292
  357.2 161.9 %copy-start.10 = (f32[1,1,1024]{2,1,0:T(1,128)S(1)}, f32[1,1,1024]{2,1,0:T(1,128)}, u32[]{:S(2)}) copy-start(f32[1,1,1024]{2,1,0:T(1,128)} %copy-done.9) | copy-start | bytes 12292
  357.2 161.9 %copy-start.12 = (f32[1,1,1024]{2,1,0:T(1,128)S(1)}, f32[1,1,1024]{2,1,0:T(1,128)}, u32[]{:S(2)}) copy-start(f32[1,1,1024]{2,1,0:T(1,128)} %copy-done.11) | copy-start | bytes 12292
Sparse Core Ops, SparseCore 0:
  11.7 115.5 all-gather.4
  360.9 121.2 reduce-scatter.1

commit v2 on v1

--- a/solution.py
+++ b/solution.py
@@ -13,6 +13,34 @@
 loss_scale = 16.0
 neg_fill = -1e30
 norm_eps = 1e-06
+
+
+def gathered(block, axis, bits):
+    size = lax.axis_size(axis)
+    index = lax.axis_index(axis)
+    held = block[None]
+    for bit in bits:
+        partner = [(i, i ^ (1 << bit)) for i in range(size)]
+        other = lax.ppermute(held, axis, partner)
+        upper = ((index >> bit) & 1) == 1
+        held = jnp.stack([jnp.where(upper, other, held), jnp.where(upper, held, other)])
+    order = sorted(range(len(bits)), key=lambda k: -bits[k])
+    held = jnp.transpose(held, [len(bits) - 1 - k for k in order] + list(range(len(bits), held.ndim)))
+    return held.reshape((size,) + block.shape)
+
+
+def scattered_sum(rows, axis, bits):
+    size = lax.axis_size(axis)
+    index = lax.axis_index(axis)
+    held = rows.reshape((size, rows.shape[0] // size) + rows.shape[1:])
+    for bit in bits:
+        held = held.reshape((held.shape[0] // 2, 2) + held.shape[1:])
+        upper = ((index >> bit) & 1) == 1
+        keep = jnp.where(upper, held[:, 1], held[:, 0])
+        send = jnp.where(upper, held[:, 0], held[:, 1])
+        partner = [(i, i ^ (1 << bit)) for i in range(size)]
+        held = keep + lax.ppermute(send, axis, partner)
+    return held[0]
 
 
 def slot_norm(raw_rows):
@@ -83,8 +111,8 @@
     decay_rate = keep_flag * ret_row
     carried = keep_flag * (1.0 - ret_row) * written + (1.0 - keep_flag) * mem_init
 
-    chain_terms = lax.all_gather(
-        jnp.concatenate([carried, decay_rate[None]], axis=0), "seg", axis=0, tiled=False
+    chain_terms = gathered(
+        jnp.concatenate([carried, decay_rate[None]], axis=0), "seg", (3, 2, 1, 0)
     )
     all_carried = chain_terms[:, :mem_rows]
     all_decay = chain_terms[:, mem_rows]
@@ -122,7 +150,9 @@
 
     running, _ = lax.scan(one_block, starting, (key_blocks, value_blocks, block_first))
 
-    memory_all = lax.all_gather(memory_in.astype(jnp.bfloat16), "tok", axis=0, tiled=True)
+    memory_all = gathered(memory_in.astype(jnp.bfloat16), "tok", (4, 3, 2, 1, 0)).reshape(
+        -1, 2 * width_kv
+    )
     mem_keys = memory_all[:, :width_kv].reshape(-1, KVH, HD)
     mem_vals = memory_all[:, width_kv:].reshape(-1, KVH, HD)
     mem_scores = (
@@ -168,9 +198,9 @@
     grad_slots = jnp.concatenate(
         [grad_keys.reshape(-1, width_kv), grad_vals.reshape(-1, width_kv)], axis=1
     )
-    local_grad = lax.psum_scatter(grad_slots, "tok", scatter_dimension=0, tiled=True)
-
-    all_local = lax.all_gather(local_grad, "seg", axis=0, tiled=False)
+    local_grad = scattered_sum(grad_slots, "tok", (0, 1, 2, 3, 4))
+
+    all_local = gathered(local_grad, "seg", (3, 2, 1, 0))
     memory_grad = all_local[seg_count - 1]
     for step in range(seg_count - 2, -1, -1):
         earlier_grad = all_local[step] + all_decay[step] * memory_grad

time: 528 us -> 447 us (0.85)
  the two profiles are of different devices: /device:TPU:16 before, /device:TPU:2 now
where the time goes in v2:
time: 447 us; the launch traced here: 445 us
  waiting for transfers between devices  201 us (45%)
  matrix products  84.7 us (19%)
  starting transfers between devices  63.5 us (14%)
  local copies, waits for them, and re-layouts  48.6 us (11%)
  other arithmetic  31.4 us (7%)
  between operations  15.5 us (3%)
    all_gather x1, waiting for transfers between devices, shards(): lax.all_gather(jnp.concatenate([seg_keys[0], seg_values[0]], axis=1), 'to...  114 us
    ppermute x13, waiting for transfers between devices, gathered(): other = lax.ppermute(held, axis, partner)  58.4 us
    ppermute x13, starting transfers between devices, gathered(): other = lax.ppermute(held, axis, partner)  49 us
    dot_general x8, matrix products, one_block(): jnp.einsum('gjtu,ugd->tgjd', seg_weights, value_block, preferred_element_...  39.6 us
    dot_general x8, matrix products, one_block(): jnp.einsum('tgjd,ugd->gjtu', queries, key_block, preferred_element_type=j...  30.2 us
    ppermute x5, waiting for transfers between devices, scattered_sum(): held = keep + lax.ppermute(send, axis, partner)  28.1 us
    unnamed x24, local copies, waits for them, and re-layouts  25.9 us
    ppermute x5, starting transfers between devices, scattered_sum(): held = keep + lax.ppermute(send, axis, partner)  14.5 us
  transfers between devices with their start and end apart: 19, of which 17 were waited for; matrix products, arithmetic and copies ran while one was open for 29% of the time, Pallas kernels for 0%

profile of v2, /device:TPU:2, one launch (start us, length us, event | category | flops | bytes accessed | tf_op | source)
XLA Modules:
  0.0 444.8 jit_solution(12528935828330636932)
XLA Ops:
  14.6 114.2 %all-gather.2.cloned.1.call-done = bf16[4096,1024]{0,1:T(8,128)(2,1)} async-done(((bf16[128,1024]{0,1:T(8,128)(2,1)}), bf16[4096,1024]{0,1:T(8,128)(2,1)}) %all-gather.2.cloned.1.call-update) | async-done | bytes 8388624 | tf_op jit(solution)/shard_map/all_gather | solution.py:77
  128.8 6.0 %fusion.132 = (bf16[4096,512]{0,1:T(8,128)(2,1)}, bf16[4096,512]{0,1:T(8,128)(2,1)}) fusion(bf16[4096,1024]{0,1:T(8,128)(2,1)} %all-gather.2.cloned.1.call-done), kind=kLoop, calls=%fused_computation.242 | loop fusion | bytes 16777216 | tf_op jit(solution)/shard_map/slice | solution.py:81
  134.8 3.1 fusion.135
  137.9 3.5 fusion.46
  142.8 8.0 %collective-permute-start = (f32[1,9,1024]{2,1,0:T(8,128)S(1)}, f32[1,9,1024]{2,1,0:T(8,128)S(1)}, u32[]{:S(2)}, u32[]{:S(2)}) collective-permute-start(f32[1,9,1024]{2,1,0:T(8,128)S(1)} %maximum_bitcast_fusion.2), channel_id=1, source_target_pairs={{0,256},{32,288},{64,320},{96,352},{128,384},{160,416},{192,448},{... | collective-permute-start | bytes 110600 | tf_op jit(solution)/shard_map/ppermute | solution.py:24
  150.8 2.6 collective-permute-done
  153.5 5.6 %collective-permute-start.1 = (f32[2,1,9,1024]{3,2,0,1:T(8,128)S(1)}, f32[2,1,9,1024]{3,2,0,1:T(8,128)S(1)}, u32[]{:S(2)}, u32[]{:S(2)}) collective-permute-start(f32[2,1,9,1024]{3,2,0,1:T(8,128)S(1)} %fusion.75), channel_id=1, source_target_pairs={{0,128},{32,160},{64,192},{96,224},{128,0},{160,32},{192,64},{224,... | collective-permute-start | bytes 221192 | tf_op jit(solution)/shard_map/ppermute | solution.py:24
  159.1 5.1 %collective-permute-done.1 = f32[2,1,9,1024]{3,2,0,1:T(8,128)S(1)} collective-permute-done((f32[2,1,9,1024]{3,2,0,1:T(8,128)S(1)}, f32[2,1,9,1024]{3,2,0,1:T(8,128)S(1)}, u32[]{:S(2)}, u32[]{:S(2)}) %collective-permute-start.1) | collective-permute-done | bytes 73760 | tf_op jit(solution)/shard_map/ppermute | solution.py:24
  164.3 2.2 collective-permute-start.2
  166.5 7.6 %collective-permute-done.2 = f32[2,2,1,9,1024]{4,3,1,0,2:T(8,128)S(1)} collective-permute-done((f32[2,2,1,9,1024]{4,3,1,0,2:T(8,128)S(1)}, f32[2,2,1,9,1024]{4,3,1,0,2:T(8,128)S(1)}, u32[]{:S(2)}, u32[]{:S(2)}) %collective-permute-start.2) | collective-permute-done | bytes 147488 | tf_op jit(solution)/shard_map/ppermute | solution.py:24
  174.2 3.4 collective-permute-start.3
  177.6 11.1 %collective-permute-done.3 = f32[2,2,2,1,9,1024]{5,4,2,1,0,3:T(8,128)S(1)} collective-permute-done((f32[2,2,2,1,9,1024]{5,4,2,1,0,3:T(8,128)S(1)}, f32[2,2,2,1,9,1024]{5,4,2,1,0,3:T(8,128)S(1)}, u32[]{:S(2)}, u32[]{:S(2)}) %collective-permute-start.3) | collective-permute-done | bytes 294944 | tf_op jit(solution)/shard_map/ppermute | solution.py:24
  189.9 3.3 collective-permute-start.4
  193.2 3.8 collective-permute-done.4
  197.0 4.5 %collective-permute-start.5 = (bf16[2,1,8,1024]{3,2,0,1:T(8,128)(2,1)S(1)}, bf16[2,1,8,1024]{3,2,0,1:T(8,128)(2,1)S(1)}, u32[]{:S(2)}, u32[]{:S(2)}) collective-permute-start(bf16[2,1,8,1024]{3,2,0,1:T(8,128)(2,1)S(1)} %pad_maximum_fusion.12), channel_id=1, source_target_pairs={{0,8},{1,9},{2,10},{3,11},{4,12},{5,13},{6,14},{7,15},{8,0},{9,1},... | collective-permute-start | bytes 98312 | tf_op jit(solution)/shard_map/ppermute | solution.py:24
  201.5 5.2 %collective-permute-done.5 = bf16[2,1,8,1024]{3,2,0,1:T(8,128)(2,1)S(1)} collective-permute-done((bf16[2,1,8,1024]{3,2,0,1:T(8,128)(2,1)S(1)}, bf16[2,1,8,1024]{3,2,0,1:T(8,128)(2,1)S(1)}, u32[]{:S(2)}, u32[]{:S(2)}) %collective-permute-start.5) | collective-permute-done | bytes 32800 | tf_op jit(solution)/shard_map/ppermute | solution.py:24
  206.7 2.0 collective-permute-start.6
  208.8 5.1 %collective-permute-done.6 = bf16[2,2,1,8,1024]{4,3,0,1,2:T(8,128)(2,1)S(1)} collective-permute-done((bf16[2,2,1,8,1024]{4,3,0,1,2:T(8,128)(2,1)S(1)}, bf16[2,2,1,8,1024]{4,3,0,1,2:T(8,128)(2,1)S(1)}, u32[]{:S(2)}, u32[]{:S(2)}) %collective-permute-start.6) | collective-permute-done | bytes 65568 | tf_op jit(solution)/shard_map/ppermute | solution.py:24
  213.9 4.1 collective-permute-start.7
  219.6 6.4 %copy.232 = bf16[64,8,8,512]{3,2,1,0:T(8,128)(2,1)} copy(bf16[64,8,8,512]{3,1,2,0:T(8,128)(2,1)} %bitcast.567) | data formatting | bytes 8388608
  226.0 7.9 %copy.136 = bf16[8,512,4,128]{3,1,2,0:T(8,128)(2,1)} copy(bf16[8,512,4,128]{1,0,3,2:T(8,128)(2,1)} %bitcast.568) | data formatting | bytes 8388608
  233.9 4.4 copy.233
  238.4 3.5 copy.138
  241.9 2.1 collective-permute-start.8
  244.0 100.8 %while.15 = (s32[]{:T(128)}, f32[4,4,128]{2,1,0:T(4,128)S(1)}, f32[4,4,128]{2,1,0:T(4,128)S(1)}, f32[128,4,4,128]{0,3,2,1:T(8,128)}, s32[8]{0:T(128)S(1)}, /*ind...) while((s32[]{:T(128)}, f32[4,4,128]{2,1,0:T(4,128)S(1)}, ...), condition=%wide.region_3.4_spmd.clone, body=%wide.region_0.3_spmd.clone.sunk | while | flops 551433856 | bytes 33430712 | solution.py:151
  246.8 3.8 fusion.161
  250.6 4.7 %fusion.165 = f32[128,4,4,128]{0,3,2,1:T(8,128)} fusion(f32[4,512,128,4]{2,1,3,0:T(8,128)} %get-tuple-element.265, f32[4,4,128]{2,1,0:T(4,128)S(1)} %get-tuple-element.292, pred[128,512]{0,1:T(8,128)(4,1)S(1)} %compare_and_fusion.2, f32[128,4,4,128]{0,3,2,1:T(8,128)} %get-tuple-element.282, bf16[8,512,4,128]{1,3,2,0:T(8,128)(2,1)} %get-tuple-element.299, ...), kind=kOutput, calls=%fused_computation.9.clone.1 | convolution fusion | flops 274464768 | bytes 6898177 | tf_op jit(solution)/shard_map/while/body/eval_jaxpr/gjtu,ugd->tgjd/dot_general | solution.py:146
  259.1 3.8 fusion.161
  262.9 5.0 %fusion.165 = f32[128,4,4,128]{0,3,2,1:T(8,128)} fusion(f32[4,512,128,4]{2,1,3,0:T(8,128)} %get-tuple-element.265, f32[4,4,128]{2,1,0:T(4,128)S(1)} %get-tuple-element.292, pred[128,512]{0,1:T(8,128)(4,1)S(1)} %compare_and_fusion.2, f32[128,4,4,128]{0,3,2,1:T(8,128)} %get-tuple-element.282, bf16[8,512,4,128]{1,3,2,0:T(8,128)(2,1)} %get-tuple-element.299, ...), kind=kOutput, calls=%fused_computation.9.clone.1 | convolution fusion | flops 274464768 | bytes 6898177 | tf_op jit(solution)/shard_map/while/body/eval_jaxpr/gjtu,ugd->tgjd/dot_general | solution.py:146
  271.8 3.8 fusion.161
  275.6 5.0 %fusion.165 = f32[128,4,4,128]{0,3,2,1:T(8,128)} fusion(f32[4,512,128,4]{2,1,3,0:T(8,128)} %get-tuple-element.265, f32[4,4,128]{2,1,0:T(4,128)S(1)} %get-tuple-element.292, pred[128,512]{0,1:T(8,128)(4,1)S(1)} %compare_and_fusion.2, f32[128,4,4,128]{0,3,2,1:T(8,128)} %get-tuple-element.282, bf16[8,512,4,128]{1,3,2,0:T(8,128)(2,1)} %get-tuple-element.299, ...), kind=kOutput, calls=%fused_computation.9.clone.1 | convolution fusion | flops 274464768 | bytes 6898177 | tf_op jit(solution)/shard_map/while/body/eval_jaxpr/gjtu,ugd->tgjd/dot_general | solution.py:146
  284.4 3.8 fusion.161
  288.2 5.0 %fusion.165 = f32[128,4,4,128]{0,3,2,1:T(8,128)} fusion(f32[4,512,128,4]{2,1,3,0:T(8,128)} %get-tuple-element.265, f32[4,4,128]{2,1,0:T(4,128)S(1)} %get-tuple-element.292, pred[128,512]{0,1:T(8,128)(4,1)S(1)} %compare_and_fusion.2, f32[128,4,4,128]{0,3,2,1:T(8,128)} %get-tuple-element.282, bf16[8,512,4,128]{1,3,2,0:T(8,128)(2,1)} %get-tuple-element.299, ...), kind=kOutput, calls=%fused_computation.9.clone.1 | convolution fusion | flops 274464768 | bytes 6898177 | tf_op jit(solution)/shard_map/while/body/eval_jaxpr/gjtu,ugd->tgjd/dot_general | solution.py:146
  297.1 3.8 fusion.161
  300.9 5.0 %fusion.165 = f32[128,4,4,128]{0,3,2,1:T(8,128)} fusion(f32[4,512,128,4]{2,1,3,0:T(8,128)} %get-tuple-element.265, f32[4,4,128]{2,1,0:T(4,128)S(1)} %get-tuple-element.292, pred[128,512]{0,1:T(8,128)(4,1)S(1)} %compare_and_fusion.2, f32[128,4,4,128]{0,3,2,1:T(8,128)} %get-tuple-element.282, bf16[8,512,4,128]{1,3,2,0:T(8,128)(2,1)} %get-tuple-element.299, ...), kind=kOutput, calls=%fused_computation.9.clone.1 | convolution fusion | flops 274464768 | bytes 6898177 | tf_op jit(solution)/shard_map/while/body/eval_jaxpr/gjtu,ugd->tgjd/dot_general | solution.py:146
  309.7 3.8 fusion.161
  313.5 5.0 %fusion.165 = f32[128,4,4,128]{0,3,2,1:T(8,128)} fusion(f32[4,512,128,4]{2,1,3,0:T(8,128)} %get-tuple-element.265, f32[4,4,128]{2,1,0:T(4,128)S(1)} %get-tuple-element.292, pred[128,512]{0,1:T(8,128)(4,1)S(1)} %compare_and_fusion.2, f32[128,4,4,128]{0,3,2,1:T(8,128)} %get-tuple-element.282, bf16[8,512,4,128]{1,3,2,0:T(8,128)(2,1)} %get-tuple-element.299, ...), kind=kOutput, calls=%fused_computation.9.clone.1 | convolution fusion | flops 274464768 | bytes 6898177 | tf_op jit(solution)/shard_map/while/body/eval_jaxpr/gjtu,ugd->tgjd/dot_general | solution.py:146
  322.3 3.8 fusion.161
  326.1 5.0 %fusion.165 = f32[128,4,4,128]{0,3,2,1:T(8,128)} fusion(f32[4,512,128,4]{2,1,3,0:T(8,128)} %get-tuple-element.265, f32[4,4,128]{2,1,0:T(4,128)S(1)} %get-tuple-element.292, pred[128,512]{0,1:T(8,128)(4,1)S(1)} %compare_and_fusion.2, f32[128,4,4,128]{0,3,2,1:T(8,128)} %get-tuple-element.282, bf16[8,512,4,128]{1,3,2,0:T(8,128)(2,1)} %get-tuple-element.299, ...), kind=kOutput, calls=%fused_computation.9.clone.1 | convolution fusion | flops 274464768 | bytes 6898177 | tf_op jit(solution)/shard_map/while/body/eval_jaxpr/gjtu,ugd->tgjd/dot_general | solution.py:146
  335.0 3.8 fusion.161
  338.8 5.0 %fusion.165 = f32[128,4,4,128]{0,3,2,1:T(8,128)} fusion(f32[4,512,128,4]{2,1,3,0:T(8,128)} %get-tuple-element.265, f32[4,4,128]{2,1,0:T(4,128)S(1)} %get-tuple-element.292, pred[128,512]{0,1:T(8,128)(4,1)S(1)} %compare_and_fusion.2, f32[128,4,4,128]{0,3,2,1:T(8,128)} %get-tuple-element.282, bf16[8,512,4,128]{1,3,2,0:T(8,128)(2,1)} %get-tuple-element.299, ...), kind=kOutput, calls=%fused_computation.9.clone.1 | convolution fusion | flops 274464768 | bytes 6898177 | tf_op jit(solution)/shard_map/while/body/eval_jaxpr/gjtu,ugd->tgjd/dot_general | solution.py:146
  345.9 1.4 bitcast_reduce_fusion
  348.9 2.0 copy.171
  351.0 2.1 concatenate.22
  353.9 2.7 fusion.136
  356.8 1.7 fusion.44
  361.3 2.5 collective-permute-start.9
  363.9 1.5 collective-permute-done.9
  365.5 1.9 collective-permute-start.10
  367.5 8.5 %collective-permute-done.10 = f32[8,8,1024]{2,1,0:T(8,128)S(1)} collective-permute-done((f32[8,8,1024]{2,1,0:T(8,128)S(1)}, f32[8,8,1024]{2,1,0:T(8,128)S(1)}, u32[]{:S(2)}, u32[]{:S(2)}) %collective-permute-start.10) | collective-permute-done | bytes 262176 | tf_op jit(solution)/shard_map/ppermute | solution.py:42
  376.1 2.6 collective-permute-start.11
  378.7 7.9 %collective-permute-done.11 = f32[4,8,1024]{2,1,0:T(8,128)S(1)} collective-permute-done((f32[4,8,1024]{2,1,0:T(8,128)S(1)}, f32[4,8,1024]{2,1,0:T(8,128)S(1)}, u32[]{:S(2)}, u32[]{:S(2)}) %collective-permute-start.11) | collective-permute-done | bytes 131104 | tf_op jit(solution)/shard_map/ppermute | solution.py:42
  386.6 4.0 collective-permute-start.12
  390.7 6.2 %collective-permute-done.12 = f32[2,8,1024]{2,1,0:T(8,128)S(1)} collective-permute-done((f32[2,8,1024]{2,1,0:T(8,128)S(1)}, f32[2,8,1024]{2,1,0:T(8,128)S(1)}, u32[]{:S(2)}, u32[]{:S(2)}) %collective-permute-start.12) | collective-permute-done | bytes 65568 | tf_op jit(solution)/shard_map/ppermute | solution.py:42
  396.9 3.4 collective-permute-start.13
  400.2 3.9 collective-permute-done.13
  404.2 6.5 %collective-permute-start.14 = (f32[1,8,1024]{2,1,0:T(8,128)S(1)}, f32[1,8,1024]{2,1,0:T(8,128)S(1)}, u32[]{:S(2)}, u32[]{:S(2)}) collective-permute-start(f32[1,8,1024]{2,1,0:T(8,128)S(1)} %bitcast_add_fusion.2), channel_id=1, source_target_pairs={{0,256},{32,288},{64,320},{96,352},{128,384},{160,416},{192,448},{... | collective-permute-start | bytes 98312 | tf_op jit(solution)/shard_map/ppermute | solution.py:24
  410.7 3.5 collective-permute-done.14
  414.3 1.9 collective-permute-start.15
  416.2 5.6 %collective-permute-done.15 = f32[2,1,8,1024]{3,2,0,1:T(8,128)S(1)} collective-permute-done((f32[2,1,8,1024]{3,2,0,1:T(8,128)S(1)}, f32[2,1,8,1024]{3,2,0,1:T(8,128)S(1)}, u32[]{:S(2)}, u32[]{:S(2)}) %collective-permute-start.15) | collective-permute-done | bytes 65568 | tf_op jit(solution)/shard_map/ppermute | solution.py:24
  421.8 1.9 collective-permute-start.16
  423.8 4.9 %collective-permute-done.16 = f32[2,2,1,8,1024]{4,3,1,0,2:T(8,128)S(1)} collective-permute-done((f32[2,2,1,8,1024]{4,3,1,0,2:T(8,128)S(1)}, f32[2,2,1,8,1024]{4,3,1,0,2:T(8,128)S(1)}, u32[]{:S(2)}, u32[]{:S(2)}) %collective-permute-start.16) | collective-permute-done | bytes 131104 | tf_op jit(solution)/shard_map/ppermute | solution.py:24
  428.8 3.4 collective-permute-start.17
  433.2 3.8 collective-permute-done.17
  (186 shorter events, 50.2 us)
Async XLA Ops:
  7.2 127.6 %copy-start = (bf16[8,512]{1,0:T(8,128)(2,1)S(1)}, bf16[8,512]{1,0:T(8,128)(2,1)}, u32[]{:S(2)}) copy-start(bf16[8,512]{1,0:T(8,128)(2,1)} %param.16) | copy-start | bytes 24580
  7.2 121.6 %all-gather.2.cloned.1.call-start = ((), (), s32[]{:S(2)}) async-start(), calls=%async_computation | async-start | bytes 8650752 | tf_op jit(solution)/shard_map/all_gather | solution.py:77
  137.9 3.5 copy-start.2
  137.9 4.8 %copy-start.7 = (f32[8,1024]{1,0:T(8,128)S(1)}, f32[8,1024]{1,0:T(8,128)}, u32[]{:S(2)}) copy-start(f32[8,1024]{1,0:T(8,128)} %param.15) | copy-start | bytes 98308
  142.8 10.6 %collective-permute-start = (f32[1,9,1024]{2,1,0:T(8,128)S(1)}, f32[1,9,1024]{2,1,0:T(8,128)S(1)}, u32[]{:S(2)}, u32[]{:S(2)}) collective-permute-start(f32[1,9,1024]{2,1,0:T(8,128)S(1)} %maximum_bitcast_fusion.2), channel_id=1, source_target_pairs={{0,256},{32,288},{64,320},{96,352},{128,384},{160,416},{192,448},{... | collective-permute-start | bytes 110600 | tf_op jit(solution)/shard_map/ppermute | solution.py:24
  153.5 10.7 %collective-permute-start.1 = (f32[2,1,9,1024]{3,2,0,1:T(8,128)S(1)}, f32[2,1,9,1024]{3,2,0,1:T(8,128)S(1)}, u32[]{:S(2)}, u32[]{:S(2)}) collective-permute-start(f32[2,1,9,1024]{3,2,0,1:T(8,128)S(1)} %fusion.75), channel_id=1, source_target_pairs={{0,128},{32,160},{64,192},{96,224},{128,0},{160,32},{192,64},{224,... | collective-permute-start | bytes 221192 | tf_op jit(solution)/shard_map/ppermute | solution.py:24
  164.3 9.8 %collective-permute-start.2 = (f32[2,2,1,9,1024]{4,3,1,0,2:T(8,128)S(1)}, f32[2,2,1,9,1024]{4,3,1,0,2:T(8,128)S(1)}, u32[]{:S(2)}, u32[]{:S(2)}) collective-permute-start(f32[2,2,1,9,1024]{4,3,1,0,2:T(8,128)S(1)} %fusion.67), channel_id=1, source_target_pairs={{0,64},{32,96},{64,0},{96,32},{128,192},{160,224},{192,128},{224,1... | collective-permute-start | bytes 442376 | tf_op jit(solution)/shard_map/ppermute | solution.py:24
  174.2 14.5 %collective-permute-start.3 = (f32[2,2,2,1,9,1024]{5,4,2,1,0,3:T(8,128)S(1)}, f32[2,2,2,1,9,1024]{5,4,2,1,0,3:T(8,128)S(1)}, u32[]{:S(2)}, u32[]{:S(2)}) collective-permute-start(f32[2,2,2,1,9,1024]{5,4,2,1,0,3:T(8,128)S(1)} %fusion.57), channel_id=1, source_target_pairs={{0,32},{32,0},{64,96},{96,64},{128,160},{160,128},{192,224},{224,1... | collective-permute-start | bytes 884744 | tf_op jit(solution)/shard_map/ppermute | solution.py:24
  177.6 40.5 %copy-start.3 = (bf16[1,128,2048]{2,1,0:T(8,128)(2,1)S(1)}, bf16[1,128,2048]{2,1,0:T(8,128)(2,1)}, u32[]{:S(2)}) copy-start(bf16[1,128,2048]{2,1,0:T(8,128)(2,1)} %param.11) | copy-start | bytes 1572868
  188.8 29.9 %copy-start.4 = (bf16[1,128,2048]{2,1,0:T(8,128)(2,1)S(1)}, bf16[1,128,2048]{2,1,0:T(8,128)(2,1)}, u32[]{:S(2)}) copy-start(bf16[1,128,2048]{2,1,0:T(8,128)(2,1)} %param.14) | copy-start | bytes 1572868
  189.9 7.1 %collective-permute-start.4 = (bf16[1,8,1024]{2,1,0:T(8,128)(2,1)S(1)}, bf16[1,8,1024]{2,1,0:T(8,128)(2,1)S(1)}, u32[]{:S(2)}, u32[]{:S(2)}) collective-permute-start(bf16[1,8,1024]{2,1,0:T(8,128)(2,1)S(1)} %get-tuple-element.149), channel_id=1, source_target_pairs={{0,16},{1,17},{2,18},{3,19},{4,20},{5,21},{6,22},{7,23},{8,24},{9,... | collective-permute-start | bytes 49160 | tf_op jit(solution)/shard_map/ppermute | solution.py:24
  197.0 9.7 %collective-permute-start.5 = (bf16[2,1,8,1024]{3,2,0,1:T(8,128)(2,1)S(1)}, bf16[2,1,8,1024]{3,2,0,1:T(8,128)(2,1)S(1)}, u32[]{:S(2)}, u32[]{:S(2)}) collective-permute-start(bf16[2,1,8,1024]{3,2,0,1:T(8,128)(2,1)S(1)} %pad_maximum_fusion.12), channel_id=1, source_target_pairs={{0,8},{1,9},{2,10},{3,11},{4,12},{5,13},{6,14},{7,15},{8,0},{9,1},... | collective-permute-start | bytes 98312 | tf_op jit(solution)/shard_map/ppermute | solution.py:24
  206.7 7.2 %collective-permute-start.6 = (bf16[2,2,1,8,1024]{4,3,0,1,2:T(8,128)(2,1)S(1)}, bf16[2,2,1,8,1024]{4,3,0,1,2:T(8,128)(2,1)S(1)}, u32[]{:S(2)}, u32[]{:S(2)}) collective-permute-start(bf16[2,2,1,8,1024]{4,3,0,1,2:T(8,128)(2,1)S(1)} %pad_maximum_fusion.9), channel_id=1, source_target_pairs={{0,4},{1,5},{2,6},{3,7},{4,0},{5,1},{6,2},{7,3},{8,12},{9,13},{10,... | collective-permute-start | bytes 196616 | tf_op jit(solution)/shard_map/ppermute | solution.py:24
  213.9 27.9 %collective-permute-start.7 = (bf16[2,2,2,1,8,1024]{5,4,0,1,2,3:T(8,128)(2,1)S(1)}, bf16[2,2,2,1,8,1024]{5,4,0,1,2,3:T(8,128)(2,1)S(1)}, u32[]{:S(2)}, u32[]{:S(2)}) collective-permute-start(bf16[2,2,2,1,8,1024]{5,4,0,1,2,3:T(8,128)(2,1)S(1)} %pad_maximum_fusion.7), channel_id=1, source_target_pairs={{0,2},{1,3},{2,0},{3,1},{4,6},{5,7},{6,4},{7,5},{8,10},{9,11},{10,... | collective-permute-start | bytes 393224 | tf_op jit(solution)/shard_map/ppermute | solution.py:24
  241.9 103.0 %collective-permute-start.8 = (bf16[2,2,2,2,1,8,1024]{6,5,0,1,2,3,4:T(8,128)(2,1)S(1)}, bf16[2,2,2,2,1,8,1024]{6,5,0,1,2,3,4:T(8,128)(2,1)S(1)}, u32[]{:S(2)}, u32[]{:S(2)}) collective-permute-start(bf16[2,2,2,2,1,8,1024]{6,5,0,1,2,3,4:T(8,128)(2,1)S(1)} %pad_maximum_fusion.4), channel_id=1, source_target_pairs={{0,1},{1,0},{2,3},{3,2},{4,5},{5,4},{6,7},{7,6},{8,9},{9,8},{10,11... | collective-permute-start | bytes 786440 | tf_op jit(solution)/shard_map/ppermute | solution.py:24
  250.6 4.7 %copy-start.1 = (f32[4,512,128,4]{2,1,3,0:T(8,128)S(1)}, f32[4,512,128,4]{2,1,3,0:T(8,128)}, u32[]{:S(2)}) copy-start(f32[4,512,128,4]{2,1,3,0:T(8,128)} %get-tuple-element.265) | copy-start | bytes 12582916 | tf_op jit(solution)/shard_map/while
  262.9 5.0 %copy-start.1 = (f32[4,512,128,4]{2,1,3,0:T(8,128)S(1)}, f32[4,512,128,4]{2,1,3,0:T(8,128)}, u32[]{:S(2)}) copy-start(f32[4,512,128,4]{2,1,3,0:T(8,128)} %get-tuple-element.265) | copy-start | bytes 12582916 | tf_op jit(solution)/shard_map/while
  275.6 5.0 %copy-start.1 = (f32[4,512,128,4]{2,1,3,0:T(8,128)S(1)}, f32[4,512,128,4]{2,1,3,0:T(8,128)}, u32[]{:S(2)}) copy-start(f32[4,512,128,4]{2,1,3,0:T(8,128)} %get-tuple-element.265) | copy-start | bytes 12582916 | tf_op jit(solution)/shard_map/while
  288.2 5.0 %copy-start.1 = (f32[4,512,128,4]{2,1,3,0:T(8,128)S(1)}, f32[4,512,128,4]{2,1,3,0:T(8,128)}, u32[]{:S(2)}) copy-start(f32[4,512,128,4]{2,1,3,0:T(8,128)} %get-tuple-element.265) | copy-start | bytes 12582916 | tf_op jit(solution)/shard_map/while
  300.9 5.0 %copy-start.1 = (f32[4,512,128,4]{2,1,3,0:T(8,128)S(1)}, f32[4,512,128,4]{2,1,3,0:T(8,128)}, u32[]{:S(2)}) copy-start(f32[4,512,128,4]{2,1,3,0:T(8,128)} %get-tuple-element.265) | copy-start | bytes 12582916 | tf_op jit(solution)/shard_map/while
  313.5 5.0 %copy-start.1 = (f32[4,512,128,4]{2,1,3,0:T(8,128)S(1)}, f32[4,512,128,4]{2,1,3,0:T(8,128)}, u32[]{:S(2)}) copy-start(f32[4,512,128,4]{2,1,3,0:T(8,128)} %get-tuple-element.265) | copy-start | bytes 12582916 | tf_op jit(solution)/shard_map/while
  326.1 5.0 %copy-start.1 = (f32[4,512,128,4]{2,1,3,0:T(8,128)S(1)}, f32[4,512,128,4]{2,1,3,0:T(8,128)}, u32[]{:S(2)}) copy-start(f32[4,512,128,4]{2,1,3,0:T(8,128)} %get-tuple-element.265) | copy-start | bytes 12582916 | tf_op jit(solution)/shard_map/while
  338.8 5.0 %copy-start.1 = (f32[4,512,128,4]{2,1,3,0:T(8,128)S(1)}, f32[4,512,128,4]{2,1,3,0:T(8,128)}, u32[]{:S(2)}) copy-start(f32[4,512,128,4]{2,1,3,0:T(8,128)} %get-tuple-element.265) | copy-start | bytes 12582916 | tf_op jit(solution)/shard_map/while
  353.9 2.9 copy-start.6
  361.3 70.9 %copy-start.5 = (bf16[128,4,4,128]{0,3,2,1:T(8,128)(2,1)S(1)}, bf16[128,4,4,128]{0,3,2,1:T(8,128)(2,1)}, u32[]{:S(2)}) copy-start(bf16[128,4,4,128]{0,3,2,1:T(8,128)(2,1)} %get-tuple-element.194) | copy-start | bytes 1572868
  361.3 4.1 collective-permute-start.9
  365.5 10.5 %collective-permute-start.10 = (f32[8,8,1024]{2,1,0:T(8,128)S(1)}, f32[8,8,1024]{2,1,0:T(8,128)S(1)}, u32[]{:S(2)}, u32[]{:S(2)}) collective-permute-start(f32[8,8,1024]{2,1,0:T(8,128)S(1)} %select_bitcast_fusion.3), channel_id=1, source_target_pairs={{0,2},{1,3},{2,0},{3,1},{4,6},{5,7},{6,4},{7,5},{8,10},{9,11},{10,... | collective-permute-start | bytes 786440 | tf_op jit(solution)/shard_map/ppermute | solution.py:42
  376.1 10.5 %collective-permute-start.11 = (f32[4,8,1024]{2,1,0:T(8,128)S(1)}, f32[4,8,1024]{2,1,0:T(8,128)S(1)}, u32[]{:S(2)}, u32[]{:S(2)}) collective-permute-start(f32[4,8,1024]{2,1,0:T(8,128)S(1)} %select_bitcast_fusion.8), channel_id=1, source_target_pairs={{0,4},{1,5},{2,6},{3,7},{4,0},{5,1},{6,2},{7,3},{8,12},{9,13},{10,... | collective-permute-start | bytes 393224 | tf_op jit(solution)/shard_map/ppermute | solution.py:42
  386.6 10.2 %collective-permute-start.12 = (f32[2,8,1024]{2,1,0:T(8,128)S(1)}, f32[2,8,1024]{2,1,0:T(8,128)S(1)}, u32[]{:S(2)}, u32[]{:S(2)}) collective-permute-start(f32[2,8,1024]{2,1,0:T(8,128)S(1)} %select_bitcast_fusion.13), channel_id=1, source_target_pairs={{0,8},{1,9},{2,10},{3,11},{4,12},{5,13},{6,14},{7,15},{8,0},{9,1},... | collective-permute-start | bytes 196616 | tf_op jit(solution)/shard_map/ppermute | solution.py:42
  396.9 7.3 %collective-permute-start.13 = (f32[1,8,1024]{2,1,0:T(8,128)S(1)}, f32[1,8,1024]{2,1,0:T(8,128)S(1)}, u32[]{:S(2)}, u32[]{:S(2)}) collective-permute-start(f32[1,8,1024]{2,1,0:T(8,128)S(1)} %select_bitcast_fusion.20), channel_id=1, source_target_pairs={{0,16},{1,17},{2,18},{3,19},{4,20},{5,21},{6,22},{7,23},{8,24},{9,... | collective-permute-start | bytes 98312 | tf_op jit(solution)/shard_map/ppermute | solution.py:42
  404.2 10.0 %collective-permute-start.14 = (f32[1,8,1024]{2,1,0:T(8,128)S(1)}, f32[1,8,1024]{2,1,0:T(8,128)S(1)}, u32[]{:S(2)}, u32[]{:S(2)}) collective-permute-start(f32[1,8,1024]{2,1,0:T(8,128)S(1)} %bitcast_add_fusion.2), channel_id=1, source_target_pairs={{0,256},{32,288},{64,320},{96,352},{128,384},{160,416},{192,448},{... | collective-permute-start | bytes 98312 | tf_op jit(solution)/shard_map/ppermute | solution.py:24
  414.3 7.5 %collective-permute-start.15 = (f32[2,1,8,1024]{3,2,0,1:T(8,128)S(1)}, f32[2,1,8,1024]{3,2,0,1:T(8,128)S(1)}, u32[]{:S(2)}, u32[]{:S(2)}) collective-permute-start(f32[2,1,8,1024]{3,2,0,1:T(8,128)S(1)} %fusion.78), channel_id=1, source_target_pairs={{0,128},{32,160},{64,192},{96,224},{128,0},{160,32},{192,64},{224,... | collective-permute-start | bytes 196616 | tf_op jit(solution)/shard_map/ppermute | solution.py:24
  421.8 6.9 %collective-permute-start.16 = (f32[2,2,1,8,1024]{4,3,1,0,2:T(8,128)S(1)}, f32[2,2,1,8,1024]{4,3,1,0,2:T(8,128)S(1)}, u32[]{:S(2)}, u32[]{:S(2)}) collective-permute-start(f32[2,2,1,8,1024]{4,3,1,0,2:T(8,128)S(1)} %fusion.74), channel_id=1, source_target_pairs={{0,64},{32,96},{64,0},{96,32},{128,192},{160,224},{192,128},{224,1... | collective-permute-start | bytes 393224 | tf_op jit(solution)/shard_map/ppermute | solution.py:24
  428.8 8.3 %collective-permute-start.17 = (f32[2,2,2,1,8,1024]{5,4,2,1,0,3:T(8,128)S(1)}, f32[2,2,2,1,8,1024]{5,4,2,1,0,3:T(8,128)S(1)}, u32[]{:S(2)}, u32[]{:S(2)}) collective-permute-start(f32[2,2,2,1,8,1024]{5,4,2,1,0,3:T(8,128)S(1)} %fusion.66), channel_id=1, source_target_pairs={{0,32},{32,0},{64,96},{96,64},{128,160},{160,128},{192,224},{224,1... | collective-permute-start | bytes 786440 | tf_op jit(solution)/shard_map/ppermute | solution.py:24
Sparse Core Ops, SparseCore 0:
  11.7 117.0 all-gather.1
